TPU v7x, 128 devices: a whole 4x4x4 slice. The times are simulated.
128 devices in a mesh: outer: 8 (over z, core), inner: 16 (over x, y).
Axes of the slice: x: 4, y: 4, z: 4, core: 2. Of those that a mesh axis runs over, the one named last changes fastest.
Arguments:
- child_update: float32 [8, 2048, 2048], P('outer', 'inner'), may hold values from -1 to 8, as said below
- block_map: int32 [2, 8, 16], replicated, may hold values from 0 to 23, as said below
- obs_design: bfloat16 [262144, 128], P(('outer', 'inner')), may hold values from -2 to 2
- obs_target: int32 [262144], P(('outer', 'inner')), may hold values from 0 to 47
Outputs:
- pivot_factor: float32 [2, 8, 1024, 1024], P(None, 'outer', 'inner')
- border_factor: float32 [2, 8, 2048, 1024], P(None, 'outer', 'inner')
- top_update: float32 [8, 2048, 2048], P('outer', 'inner')
Inputs may be any that keep to these rules, and one draw needn't show every extreme that they name: `child_update`: each group's matrix is symmetric and positive definite. `block_map`: entry [l, g] names distinct parent blocks for the blocks of one child; groups under the same child hold equal entries; the two children of a parent together name every parent block.
All inputs are finite; a program needn't handle non-finite values.
Results may differ from a plain program's by a relative error of at most 0.0003.
Values sent between devices are 32-bit elements; how exact they have to be, the bound alone decides.
No kernel may reach another device: no remote copies, remote signals or barrier semaphores. Data moves between devices by JAX's collectives and lax.ppermute only.
A program may use at most 128 MiB of HBM per device.

v0:
```python
import math
import jax
import jax.numpy as jnp
from jax import lax
from jax.sharding import PartitionSpec as P

S = 1024
B = 2048
BLK = 128
LEVELS = 2
HIGHEST = lax.Precision.HIGHEST


def partner_2(block, axis, bit):
    count = lax.axis_size(axis)
    route = []
    for low in range(count):
        high = low | 1 << bit
        if high != low and high < count:
            route += [(low, high), (high, low)]
    return lax.ppermute(block, axis, route)


def block_source(child_map, parent_count):
    child_count = child_map.shape[0]
    matches = child_map[:, None] == jnp.arange(parent_count, dtype=jnp.int32)[None, :]
    source = jnp.sum(
        jnp.where(matches, jnp.arange(child_count, dtype=jnp.int32)[:, None], 0), axis=0
    )
    present = jnp.any(matches, axis=0)
    return (source, present)


def parent_columns(child_rows, child_map, parent_count):
    row_count = child_rows.shape[0]
    child_count = child_map.shape[0]
    block_size = child_rows.shape[1] // child_count
    source, present = block_source(child_map, parent_count)
    blocks = child_rows.reshape(row_count, child_count, block_size)
    picked = jnp.take(blocks, source, axis=1)
    picked = jnp.where(present[None, :, None], picked, jnp.zeros_like(picked))
    return picked.reshape(row_count, parent_count * block_size)


def parent_rows(child_cols, child_map, parent_count):
    col_count = child_cols.shape[1]
    child_count = child_map.shape[0]
    block_size = child_cols.shape[0] // child_count
    source, present = block_source(child_map, parent_count)
    blocks = child_cols.reshape(child_count, block_size, col_count)
    picked = jnp.take(blocks, source, axis=0)
    picked = jnp.where(present[:, None, None], picked, jnp.zeros_like(picked))
    return picked.reshape(parent_count * block_size, col_count)


def owner_major(parent_cols, inner_count):
    row_count = parent_cols.shape[0]
    sep_part = parent_cols[:, :S].reshape(row_count, inner_count, S // inner_count)
    border_part = parent_cols[:, S:].reshape(row_count, inner_count, B // inner_count)
    return jnp.concatenate([sep_part, border_part], axis=2)


def blocked_cholesky(matrix, panel_size):
    order = matrix.shape[0]
    lower_factor = jnp.zeros_like(matrix)
    trailing = matrix
    inverse_list = []
    for panel_index in range(order // panel_size):
        first = panel_index * panel_size
        last = first + panel_size
        diagonal_block = trailing[first:last, first:last]
        panel_lower = jnp.linalg.cholesky(diagonal_block)
        identity = jnp.eye(panel_size, dtype=jnp.float32)
        inverse = jax.scipy.linalg.solve_triangular(panel_lower, identity, lower=True)
        inverse_list.append(inverse)
        lower_factor = lower_factor.at[first:last, first:last].set(panel_lower)
        if last < order:
            below = jnp.dot(
                trailing[last:, first:last],
                inverse.T,
                precision=HIGHEST,
                preferred_element_type=jnp.float32,
            )
            lower_factor = lower_factor.at[last:, first:last].set(below)
            update = jnp.dot(below, below.T, precision=HIGHEST, preferred_element_type=jnp.float32)
            trailing = trailing.at[last:, last:].add(-update)
    return (lower_factor, inverse_list)


def cholesky_inverse(matrix, base_size):
    order = matrix.shape[0]
    if order <= base_size:
        lower = jnp.linalg.cholesky(matrix)
        identity = jnp.eye(order, dtype=jnp.float32)
        return (lower, jax.scipy.linalg.solve_triangular(lower, identity, lower=True))
    half = order // 2
    lower_11, inverse_11 = cholesky_inverse(matrix[:half, :half], base_size)
    lower_21 = jnp.dot(
        matrix[half:, :half], inverse_11.T, precision=HIGHEST, preferred_element_type=jnp.float32
    )
    schur = matrix[half:, half:] - jnp.dot(
        lower_21, lower_21.T, precision=HIGHEST, preferred_element_type=jnp.float32
    )
    lower_22, inverse_22 = cholesky_inverse(schur, base_size)
    inverse_21 = -jnp.dot(
        inverse_22,
        jnp.dot(lower_21, inverse_11, precision=HIGHEST, preferred_element_type=jnp.float32),
        precision=HIGHEST,
        preferred_element_type=jnp.float32,
    )
    zero = jnp.zeros((half, half), jnp.float32)
    lower = jnp.block([[lower_11, zero], [lower_21, lower_22]])
    inverse = jnp.block([[inverse_11, zero], [inverse_21, inverse_22]])
    return (lower, inverse)


def border_solve(rows_in, lower_factor, inverse_list, panel_size):
    solved = []
    for panel_index in range(len(inverse_list)):
        first = panel_index * panel_size
        pending = rows_in[:, first : first + panel_size]
        for earlier in range(panel_index):
            coupling = lower_factor[
                first : first + panel_size, earlier * panel_size : (earlier + 1) * panel_size
            ]
            pending = pending - jnp.dot(
                solved[earlier], coupling.T, precision=HIGHEST, preferred_element_type=jnp.float32
            )
        solved.append(
            jnp.dot(
                pending,
                inverse_list[panel_index].T,
                precision=HIGHEST,
                preferred_element_type=jnp.float32,
            )
        )
    return jnp.concatenate(solved, axis=1)


def shards(child_update, block_map, obs_design, obs_target):
    inner_count = lax.axis_size("inner")
    group_count = lax.axis_size("outer")
    group_index = lax.axis_index("outer")
    member = lax.axis_index("inner")
    parent_count = (S + B) // BLK
    sep_rows = S // inner_count
    sep_blocks = S // BLK
    panel_size = min(S, 256)
    front_total = sum((group_count >> level_index + 1 for level_index in range(LEVELS)))
    target_total = front_total * sep_blocks
    row_count = obs_design.shape[0]
    step_rows = math.gcd(row_count, 256)
    target_ids = jnp.arange(target_total, dtype=jnp.int32)

    def add_rows(block_index, running):
        design = lax.dynamic_slice_in_dim(obs_design, block_index * step_rows, step_rows, 0)
        labels = lax.dynamic_slice_in_dim(obs_target, block_index * step_rows, step_rows, 0)
        selector = (labels[:, None] == target_ids[None, :]).astype(jnp.bfloat16)
        spread = selector[:, :, None] * design[:, None, :]
        return running + jnp.einsum(
            "rtj,rk->tjk", spread, design, preferred_element_type=jnp.float32
        )

    gram_blocks = lax.fori_loop(
        0, row_count // step_rows, add_rows, jnp.zeros((target_total, BLK, BLK), jnp.float32)
    )
    per_front = gram_blocks.reshape(front_total, S, BLK)
    obs_share = lax.psum(
        lax.psum_scatter(per_front, "inner", scatter_dimension=1, tiled=True), "outer"
    )
    current = child_update[0]
    pivot_list = []
    border_list = []
    front_offset = 0
    block_start = member * sep_rows // BLK * BLK
    for level_index in range(LEVELS):
        partner = group_index ^ 1 << level_index
        level_maps = block_map[level_index]
        own_map = lax.dynamic_index_in_dim(level_maps, group_index, 0, keepdims=False)
        sib_map = lax.dynamic_index_in_dim(level_maps, partner, 0, keepdims=False)
        sibling = partner_2(current, "outer", level_index)
        outgoing = jnp.stack(
            [
                owner_major(parent_columns(current, own_map, parent_count), inner_count),
                owner_major(parent_columns(sibling, sib_map, parent_count), inner_count),
            ]
        )
        arrived = lax.all_to_all(outgoing, "inner", split_axis=2, concat_axis=1, tiled=True)
        own_cols = parent_rows(arrived[0, :, 0, :], own_map, parent_count)
        sib_cols = parent_rows(arrived[1, :, 0, :], sib_map, parent_count)
        front_rows = (own_cols + sib_cols).T
        front_slot = front_offset + (group_index >> level_index + 1)
        obs_rows = lax.dynamic_index_in_dim(obs_share, front_slot, 0, keepdims=False)
        sep_front = front_rows[:sep_rows]
        block_now = lax.dynamic_slice_in_dim(sep_front, block_start, BLK, 1)
        sep_front = lax.dynamic_update_slice_in_dim(sep_front, block_now + obs_rows, block_start, 1)
        front_offset = front_offset + (group_count >> level_index + 1)
        pivot_all = lax.all_gather(sep_front[:, :S], "inner", axis=0, tiled=True)
        border_front = front_rows[sep_rows:]
        coupling_all = lax.all_gather(border_front[:, :S], "inner", axis=0, tiled=True)
        pivot_lower, pivot_inverse = cholesky_inverse(pivot_all, BLK)
        border_all = jnp.dot(
            coupling_all, pivot_inverse.T, precision=HIGHEST, preferred_element_type=jnp.float32
        )
        border_factor = lax.dynamic_slice_in_dim(
            border_all, member * (B // inner_count), B // inner_count, 0
        )
        product = jnp.einsum(
            "rs,cs->rc",
            border_factor,
            border_all,
            precision=HIGHEST,
            preferred_element_type=jnp.float32,
        )
        current = border_front[:, S:] - product
        pivot_list.append(lax.dynamic_slice_in_dim(pivot_lower, member * sep_rows, sep_rows, 0))
        border_list.append(border_factor)
    pivot_factor = jnp.stack(pivot_list)[:, None]
    border_out = jnp.stack(border_list)[:, None]
    return (pivot_factor, border_out, current[None])


def solution(mesh):
    in_specs = (P("outer", "inner", None), P(), P(("outer", "inner"), None), P(("outer", "inner")))
    out_specs = (
        P(None, "outer", "inner", None),
        P(None, "outer", "inner", None),
        P("outer", "inner", None),
    )
    return jax.shard_map(shards, mesh=mesh, in_specs=in_specs, out_specs=out_specs, check_vma=False)
```

profile of v0, /device:TPU:1, one launch (start us, length us, event | category | flops | bytes accessed | tf_op | source)
XLA Modules:
  0.0 1052.3 jit_solution(1851597873496397429)
XLA Ops:
  11.1 25.9 %while.14 = (s32[]{:T(128)}, f32[48,128,128]{2,1,0:T(8,128)S(1)}, s32[2048]{0:T(1024)}, bf16[2048,128]{1,0:T(8,128)(2,1)}, s32[]{:T(128)}, /*index=5*/s32[]{:T(128)}, s32[]{:T(128)}, s32[]{:T(128)}) while((s32[]{:T(128)}, f32[48,128,128]{2,1,0:T(8,128)S(1)}, s32[2048]{0:T(1024)}, bf16[2048,128]{1,0:T(8,128)(2,1)}, s32[]{:T(128)}, ...), condition=%wide.region_5.8_spmd.clone, body=%wide.region_4.7_spmd.clone.sunk | while | flops 405823488 | bytes 6737053 | solution.py:164
  64.3 46.5 %all-to-all-done = f32[2,128,16,192]{1,3,0,2:T(8,128)S(1)} async-done(((f32[2,128,16,192]{1,3,0,2:T(8,128)}), f32[2,128,16,192]{1,3,0,2:T(8,128)S(1)}, u32[]{:S(2)}, u32[]{:S(2)}) %all-to-all-start) | async-done | bytes 3145760 | tf_op jit(solution)/shard_map/all_to_all | solution.py:188
  115.6 39.2 %reduce-scatter.2.cloned.1.call-done = f32[6,64,128]{2,0,1:T(8,128)} async-done(((f32[6,1024,128]{2,0,1:T(8,128)}), f32[6,64,128]{2,0,1:T(8,128)}) %reduce-scatter.2.cloned.1.call-update) | async-done | bytes 196624 | tf_op jit(solution)/shard_map/reduce_scatter | solution.py:169
  157.8 58.7 %all-reduce.30.cloned.1.call-done = f32[6,64,128]{2,0,1:T(8,128)} async-done(((f32[6,64,128]{2,0,1:T(8,128)}), f32[6,64,128]{2,0,1:T(8,128)}) %all-reduce.30.cloned.1.call-update) | async-done | bytes 196624 | tf_op jit(solution)/shard_map/psum | solution.py:168
  221.2 50.2 %all-gather.5.cloned.1.call-done = f32[1024,1024]{1,0:T(8,128)} async-done(((f32[64,1024]{1,0:T(8,128)}), f32[1024,1024]{1,0:T(8,128)}) %all-gather.5.cloned.1.call-update) | async-done | bytes 4194320 | tf_op jit(solution)/shard_map/all_gather | solution.py:198
  273.3 11.7 %cholesky.254 = f32[128,128]{1,0:T(8,128)S(1)} custom-call(f32[128,128]{1,0:T(8,128)S(1)} %get-tuple-element.171), custom_call_target="Cholesky" | custom-call | tf_op jit(solution)/shard_map/jit(cholesky)/cholesky | solution.py:93
  298.6 11.7 %cholesky.265 = f32[128,128]{1,0:T(8,128)S(1)} custom-call(f32[128,128]{1,0:T(8,128)S(1)} %fusion.203), custom_call_target="Cholesky" | custom-call | tf_op jit(solution)/shard_map/jit(cholesky)/cholesky | solution.py:93
  326.5 11.7 %cholesky.276 = f32[128,128]{1,0:T(8,128)S(1)} custom-call(f32[128,128]{1,0:T(8,128)S(1)} %fusion.201), custom_call_target="Cholesky" | custom-call | tf_op jit(solution)/shard_map/jit(cholesky)/cholesky | solution.py:93
  350.9 11.9 %cholesky.287 = f32[128,128]{1,0:T(8,128)S(1)} custom-call(f32[128,128]{1,0:T(8,128)S(1)} %fusion.199), custom_call_target="Cholesky" | custom-call | tf_op jit(solution)/shard_map/jit(cholesky)/cholesky | solution.py:93
  391.3 12.9 %cholesky.298 = f32[128,128]{1,0:T(8,128)S(1)} custom-call(f32[128,128]{1,0:T(8,128)} %fusion.197), custom_call_target="Cholesky" | custom-call | tf_op jit(solution)/shard_map/jit(cholesky)/cholesky | solution.py:93
  406.1 11.3 %custom-call.25 = f32[1,128,128]{1,2,0:T(8,128)} custom-call(f32[1,128,128]{2,1,0:T(8,128)} %get-tuple-element.158), custom_call_target="InvertDiagBlocksLowerTriangular" | custom-call | tf_op jit(solution)/shard_map/jit(_solve_triangular)/triangular_solve | solution.py:95
  425.0 13.2 %cholesky.309 = f32[128,128]{1,0:T(8,128)} custom-call(f32[128,128]{1,0:T(8,128)} %fusion.195), custom_call_target="Cholesky" | custom-call | tf_op jit(solution)/shard_map/jit(cholesky)/cholesky | solution.py:93
  442.0 11.3 %custom-call.26 = f32[1,128,128]{1,2,0:T(8,128)} custom-call(f32[1,128,128]{2,1,0:T(8,128)} %get-tuple-element.156), custom_call_target="InvertDiagBlocksLowerTriangular" | custom-call | tf_op jit(solution)/shard_map/jit(_solve_triangular)/triangular_solve | solution.py:95
  467.4 13.3 %cholesky.320 = f32[128,128]{1,0:T(8,128)} custom-call(f32[128,128]{1,0:T(8,128)} %fusion.193), custom_call_target="Cholesky" | custom-call | tf_op jit(solution)/shard_map/jit(cholesky)/cholesky | solution.py:93
  484.5 11.3 %custom-call.27 = f32[1,128,128]{1,2,0:T(8,128)} custom-call(f32[1,128,128]{2,1,0:T(8,128)} %get-tuple-element.154), custom_call_target="InvertDiagBlocksLowerTriangular" | custom-call | tf_op jit(solution)/shard_map/jit(_solve_triangular)/triangular_solve | solution.py:95
  504.1 13.2 %cholesky.331 = f32[128,128]{1,0:T(8,128)} custom-call(f32[128,128]{1,0:T(8,128)} %fusion.191), custom_call_target="Cholesky" | custom-call | tf_op jit(solution)/shard_map/jit(cholesky)/cholesky | solution.py:93
  520.9 11.3 %custom-call.28 = f32[1,128,128]{1,2,0:T(8,128)} custom-call(f32[1,128,128]{2,1,0:T(8,128)} %get-tuple-element.152), custom_call_target="InvertDiagBlocksLowerTriangular" | custom-call | tf_op jit(solution)/shard_map/jit(_solve_triangular)/triangular_solve | solution.py:95
  546.7 36.2 %fusion.12 = f32[2048,1024]{1,0:T(8,128)S(1)} fusion(f32[2048,1024]{1,0:T(8,128)} %all-gather.7.cloned.1.call-done, f32[512,512]{1,0:T(8,128)S(1)} %copy-done.37, f32[128,128]{1,0:T(8,128)S(1)} %copy-done.85, f32[128,128]{1,0:T(8,128)} %copy-done.81, f32[128,256]{1,0:T(8,128)} %concatenate.310, f32[256,256]{1,0:T(8,128)} %copy-done.77, ...), kind=kOutput, calls=%fused_computation.29 | convolution fusion | flops 25778192384 | bytes 19922944 | tf_op jit(solution)/shard_map/dot_general | solution.py:202
  600.7 16.1 %collective-permute-done.1 = f32[128,2048]{1,0:T(8,128)} collective-permute-done((f32[128,2048]{1,0:T(8,128)}, f32[128,2048]{1,0:T(8,128)}, u32[]{:S(2)}, u32[]{:S(2)}) %collective-permute-start.1) | collective-permute-done | bytes 1048608 | tf_op jit(solution)/shard_map/ppermute | solution.py:21
  623.8 42.2 %all_to_all.30 = f32[2,128,16,192]{1,3,0,2:T(8,128)S(1)} all-to-all(f32[2,128,16,192]{1,3,0,2:T(8,128)S(1)} %pad_maximum_fusion.1), channel_id=1, replica_groups=mesh['outer'=8,'inner'=16] {'inner'}, dimensions={2} | all-to-all | bytes 6291456 | tf_op jit(solution)/shard_map/all_to_all | solution.py:188
  696.5 29.6 %all-gather.9.cloned.1.call-done = f32[1024,1024]{1,0:T(8,128)} async-done(((f32[64,1024]{1,0:T(8,128)}), f32[1024,1024]{1,0:T(8,128)}) %all-gather.9.cloned.1.call-update) | async-done | bytes 4194320 | tf_op jit(solution)/shard_map/all_gather | solution.py:198
  728.1 11.7 %cholesky.342 = f32[128,128]{1,0:T(8,128)S(1)} custom-call(f32[128,128]{1,0:T(8,128)S(1)} %get-tuple-element.169), custom_call_target="Cholesky" | custom-call | tf_op jit(solution)/shard_map/jit(cholesky)/cholesky | solution.py:93
  754.2 11.9 %cholesky.353 = f32[128,128]{1,0:T(8,128)S(1)} custom-call(f32[128,128]{1,0:T(8,128)S(1)} %fusion.187), custom_call_target="Cholesky" | custom-call | tf_op jit(solution)/shard_map/jit(cholesky)/cholesky | solution.py:93
  783.0 11.7 %cholesky.364 = f32[128,128]{1,0:T(8,128)S(1)} custom-call(f32[128,128]{1,0:T(8,128)S(1)} %fusion.185), custom_call_target="Cholesky" | custom-call | tf_op jit(solution)/shard_map/jit(cholesky)/cholesky | solution.py:93
  808.2 12.1 %cholesky.375 = f32[128,128]{1,0:T(8,128)S(1)} custom-call(f32[128,128]{1,0:T(8,128)S(1)} %fusion.183), custom_call_target="Cholesky" | custom-call | tf_op jit(solution)/shard_map/jit(cholesky)/cholesky | solution.py:93
  849.2 11.9 %cholesky.386 = f32[128,128]{1,0:T(8,128)S(1)} custom-call(f32[128,128]{1,0:T(8,128)S(1)} %fusion.181), custom_call_target="Cholesky" | custom-call | tf_op jit(solution)/shard_map/jit(cholesky)/cholesky | solution.py:93
  881.3 13.2 %cholesky.397 = f32[128,128]{1,0:T(8,128)} custom-call(f32[128,128]{1,0:T(8,128)} %fusion.179), custom_call_target="Cholesky" | custom-call | tf_op jit(solution)/shard_map/jit(cholesky)/cholesky | solution.py:93
  898.2 11.3 %custom-call.34 = f32[1,128,128]{1,2,0:T(8,128)} custom-call(f32[1,128,128]{2,1,0:T(8,128)} %get-tuple-element.140), custom_call_target="InvertDiagBlocksLowerTriangular" | custom-call | tf_op jit(solution)/shard_map/jit(_solve_triangular)/triangular_solve | solution.py:95
  924.3 12.5 %cholesky.408 = f32[128,128]{1,0:T(8,128)S(1)} custom-call(f32[128,128]{1,0:T(8,128)} %fusion.177), custom_call_target="Cholesky" | custom-call | tf_op jit(solution)/shard_map/jit(cholesky)/cholesky | solution.py:93
  956.9 13.2 %cholesky.419 = f32[128,128]{1,0:T(8,128)} custom-call(f32[128,128]{1,0:T(8,128)} %fusion.175), custom_call_target="Cholesky" | custom-call | tf_op jit(solution)/shard_map/jit(cholesky)/cholesky | solution.py:93
  974.1 11.3 %custom-call.36 = f32[1,128,128]{1,2,0:T(8,128)} custom-call(f32[1,128,128]{2,1,0:T(8,128)} %get-tuple-element.136), custom_call_target="InvertDiagBlocksLowerTriangular" | custom-call | tf_op jit(solution)/shard_map/jit(_solve_triangular)/triangular_solve | solution.py:95
  1003.8 30.6 %fusion.10 = f32[2048,1024]{1,0:T(8,128)S(1)} fusion(f32[2048,1024]{1,0:T(8,128)} %all-gather.11.cloned.1.call-done, f32[512,512]{1,0:T(8,128)S(1)} %copy-done.36, f32[128,128]{1,0:T(8,128)} %copy.496, f32[128,128]{1,0:T(8,128)} %copy-done.80, f32[128,256]{1,0:T(8,128)S(1)} %copy-done.67, f32[256,256]{1,0:T(8,128)} %copy-done.76, ...), kind=kOutput, calls=%fused_computation.23 | convolution fusion | flops 25778192384 | bytes 19922944 | tf_op jit(solution)/shard_map/dot_general | solution.py:202
  (543 shorter events, 420.4 us)
Async XLA Ops:
  7.2 147.6 %reduce-scatter.2.cloned.1.call-start = ((), (), s32[]{:S(2)}) async-start(), calls=%async_computation.3 | async-start | bytes 4456448 | tf_op jit(solution)/shard_map/reduce_scatter | solution.py:169
  9.7 38.6 %collective-permute-start = (f32[128,2048]{0,1:T(8,128)}, f32[128,2048]{0,1:T(8,128)}, u32[]{:S(2)}, u32[]{:S(2)}) collective-permute-start(f32[128,2048]{0,1:T(8,128)} %bitcast.8), channel_id=1, source_target_pairs={{0,16},{16,0},{32,48},{48,32},{64,80},{80,64},{96,112},{112,96},{1... | collective-permute-start | bytes 3145736 | tf_op jit(solution)/shard_map/ppermute | solution.py:21
  42.7 177.7 %copy-start.89 = (s32[24]{0:T(128)}, s32[24]{0:T(128)S(1)}, u32[]{:S(2)}) copy-start(s32[24]{0:T(128)S(1)} %get-tuple-element.186) | copy-start | bytes 292
  57.3 53.5 %all-to-all-start = ((f32[2,128,16,192]{1,3,0,2:T(8,128)}), f32[2,128,16,192]{1,3,0,2:T(8,128)S(1)}, u32[]{:S(2)}, u32[]{:S(2)}) async-start(f32[2,128,16,192]{1,3,0,2:T(8,128)} %pad_maximum_fusion), calls=%async_computation | async-start | bytes 6291456 | tf_op jit(solution)/shard_map/all_to_all | solution.py:188
  64.2 152.3 %all-reduce.30.cloned.1.call-start = ((), (), s32[]{:S(2)}) async-start(), calls=%async_computation.4 | async-start | bytes 524288 | tf_op jit(solution)/shard_map/psum | solution.py:168
  154.8 116.6 %all-gather.5.cloned.1.call-start = ((), (), s32[]{:S(2)}) async-start(), calls=%async_computation.5 | async-start | bytes 4456448 | tf_op jit(solution)/shard_map/all_gather | solution.py:198
  218.9 327.8 %all-gather.7.cloned.1.call-start = ((), (), s32[]{:S(2)}) async-start(), calls=%async_computation.6 | async-start | bytes 8912896 | tf_op jit(solution)/shard_map/all_gather | solution.py:200
  219.8 506.3 %all-gather.9.cloned.1.call-start = ((), (), s32[]{:S(2)}) async-start(), calls=%async_computation.7 | async-start | bytes 4456448 | tf_op jit(solution)/shard_map/all_gather | solution.py:198
  322.6 52.3 %copy-start.51 = (f32[128,128]{1,0:T(8,128)}, f32[128,128]{1,0:T(8,128)S(1)}, u32[]{:S(2)}) copy-start(f32[128,128]{1,0:T(8,128)S(1)} %copy.426) | copy-start | bytes 196612
  324.4 25.6 %copy-start.44 = (f32[128,128]{1,0:T(8,128)}, f32[128,128]{1,0:T(8,128)S(1)}, u32[]{:S(2)}) copy-start(f32[128,128]{1,0:T(8,128)S(1)} %convolution_negate_fusion.13) | copy-start | bytes 196612
  325.8 54.7 %copy-start.3 = (f32[256,256]{0,1:T(8,128)}, f32[256,256]{0,1:T(8,128)S(1)}, u32[]{:S(2)}) copy-start(f32[256,256]{0,1:T(8,128)S(1)} %fusion.133) | copy-start | bytes 786436
  350.3 29.6 %copy-start.45 = (f32[128,128]{1,0:T(8,128)S(1)}, f32[128,128]{1,0:T(8,128)}, u32[]{:S(2)}) copy-start(f32[128,128]{1,0:T(8,128)} %copy-done.44) | copy-start | bytes 196612
  350.5 30.0 %copy-start.16 = (f32[128,128]{0,1:T(8,128)}, f32[128,128]{0,1:T(8,128)S(1)}, u32[]{:S(2)}) copy-start(f32[128,128]{0,1:T(8,128)S(1)} %fusion.170) | copy-start | bytes 196612
  385.4 156.4 %copy-start.1 = (f32[512,512]{0,1:T(8,128)}, f32[512,512]{0,1:T(8,128)S(1)}, u32[]{:S(2)}) copy-start(f32[512,512]{0,1:T(8,128)S(1)} %fusion.51) | copy-start | bytes 3145732
  535.5 6.3 copy-start.23
  535.5 6.3 copy-start.27
  535.5 6.3 copy-start.32
  535.5 6.3 copy-start.57
  535.6 6.3 copy-start.61
  536.8 6.9 copy-start.65
  582.9 9.7 copy-start
  582.9 11.0 %copy-start.88 = (s32[24]{0:T(128)S(1)}, s32[24]{0:T(128)}, u32[]{:S(2)}) copy-start(s32[24]{0:T(128)} %compare_select_fusion.1) | copy-start | bytes 292
  582.9 11.0 %copy-start.90 = (s32[24]{0:T(128)S(1)}, s32[24]{0:T(128)}, u32[]{:S(2)}) copy-start(s32[24]{0:T(128)} %copy-done.89) | copy-start | bytes 292
  592.6 24.2 %collective-permute-start.1 = (f32[128,2048]{1,0:T(8,128)}, f32[128,2048]{1,0:T(8,128)}, u32[]{:S(2)}, u32[]{:S(2)}) collective-permute-start(f32[128,2048]{1,0:T(8,128)} %convolution_subtract_fusion.1), channel_id=1, source_target_pairs={{0,32},{32,0},{16,48},{48,16},{64,96},{96,64},{80,112},{112,80},{1... | collective-permute-start | bytes 3145736 | tf_op jit(solution)/shard_map/ppermute | solution.py:21
  673.7 6.8 copy-start.17
  673.7 12.4 %copy-start.2 = (f32[512,512]{0,1:T(8,128)S(1)}, f32[512,512]{0,1:T(8,128)}, u32[]{:S(2)}) copy-start(f32[512,512]{0,1:T(8,128)} %copy-done.1) | copy-start | bytes 3145732
  674.5 329.2 %all-gather.11.cloned.1.call-start = ((), (), s32[]{:S(2)}) async-start(), calls=%async_computation.8 | async-start | bytes 8912896 | tf_op jit(solution)/shard_map/all_gather | solution.py:200
  678.7 9.7 copy-start.75
  783.0 54.4 %copy-start.50 = (f32[128,128]{1,0:T(8,128)S(1)}, f32[128,128]{1,0:T(8,128)}, u32[]{:S(2)}) copy-start(f32[128,128]{1,0:T(8,128)} %copy-done.49) | copy-start | bytes 196612
  806.8 32.2 %copy-start.20 = (f32[128,256]{1,0:T(8,128)}, f32[128,256]{1,0:T(8,128)S(1)}, u32[]{:S(2)}) copy-start(f32[128,256]{1,0:T(8,128)S(1)} %concatenate.333) | copy-start | bytes 393220
  989.6 11.3 %copy-start.64 = (f32[256,512]{1,0:T(8,128)}, f32[256,512]{1,0:T(8,128)S(1)}, u32[]{:S(2)}) copy-start(f32[256,512]{1,0:T(8,128)S(1)} %concatenate.353) | copy-start | bytes 1572868
  1034.4 9.7 copy-start.15
  (68 other events, 196.5 us)
Sparse Core Ops, SparseCore 0:
  41.0 113.6 reduce-scatter.1
  157.1 59.3 all-reduce.29
  219.2 52.1 all-gather.4
  274.0 70.5 all-gather.6
  674.7 51.4 all-gather.8
  728.2 70.6 all-gather.10
where the time goes:
time: 1060 us; the launch traced here: 1050 us
  other arithmetic  460 us (43%)
  waiting for transfers between devices  241 us (23%)
  matrix products  169 us (16%)
  local copies, waits for them, and re-layouts  113 us (11%)
  blocking collectives  42.2 us (4%)
  between operations  16.8 us (2%)
    another operation x48, other arithmetic, cholesky_inverse(): lower = jnp.linalg.cholesky(matrix)  214 us
    another operation x32, other arithmetic, cholesky_inverse(): jax.scipy.linalg.solve_triangular(lower, identity, lower=True)  192 us
    all_gather x2, waiting for transfers between devices, shards(): pivot_all = lax.all_gather(sep_front[:, :S], 'inner', axis=0, tiled=True)  79.9 us
    dot_general x2, matrix products, shards(): jnp.dot(coupling_all, pivot_inverse.T, precision=HIGHEST, preferred_eleme...  66.8 us
    psum x1, waiting for transfers between devices, shards(): lax.psum(lax.psum_scatter(per_front, 'inner', scatter_dimension=1, tiled=...  58.7 us
    all_to_all x1, waiting for transfers between devices, shards(): lax.all_to_all(outgoing, 'inner', split_axis=2, concat_axis=1, tiled=True)  46.5 us
    all_to_all x1, blocking collectives, shards(): lax.all_to_all(outgoing, 'inner', split_axis=2, concat_axis=1, tiled=True)  42.2 us
    reduce_scatter x1, waiting for transfers between devices, shards(): lax.psum_scatter(per_front, 'inner', scatter_dimension=1, tiled=True)  39.2 us
  transfers between devices with their start and end apart: 9, of which 6 were waited for; matrix products, arithmetic and copies ran while one was open for 59% of the time, Pallas kernels for 0%

commit v1 on v0

--- a/solution.py
+++ b/solution.py
@@ -9,6 +9,15 @@
 BLK = 128
 LEVELS = 2
 HIGHEST = lax.Precision.HIGHEST
+
+
+def perform_windows_by_axis(lane_axis, x_in):
+    return jnp.concatenate(
+        lax.all_to_all(
+            jnp.stack([x_in for _ in range(lax.axis_size(lane_axis))], axis=0), lane_axis, 0, 0
+        ),
+        axis=0,
+    )
 
 
 def partner_2(block, axis, bit):
@@ -195,7 +204,7 @@
         block_now = lax.dynamic_slice_in_dim(sep_front, block_start, BLK, 1)
         sep_front = lax.dynamic_update_slice_in_dim(sep_front, block_now + obs_rows, block_start, 1)
         front_offset = front_offset + (group_count >> level_index + 1)
-        pivot_all = lax.all_gather(sep_front[:, :S], "inner", axis=0, tiled=True)
+        pivot_all = perform_windows_by_axis("inner", sep_front[:, :S])
         border_front = front_rows[sep_rows:]
         coupling_all = lax.all_gather(border_front[:, :S], "inner", axis=0, tiled=True)
         pivot_lower, pivot_inverse = cholesky_inverse(pivot_all, BLK)

time: 1060 us -> 1110 us (1.047)
  the two profiles are of different devices: /device:TPU:1 before, /device:TPU:96 now
where the time goes in v1:
time: 1110 us; the launch traced here: 1100 us
  other arithmetic  464 us (42%)
  waiting for transfers between devices  305 us (27%)
  matrix products  169 us (15%)
  local copies, waits for them, and re-layouts  113 us (10%)
  starting transfers between devices  31.2 us (3%)
  between operations  16.7 us (2%)
    another operation x48, other arithmetic, cholesky_inverse(): lower = jnp.linalg.cholesky(matrix)  214 us
    another operation x32, other arithmetic, cholesky_inverse(): jax.scipy.linalg.solve_triangular(lower, identity, lower=True)  192 us
    all_to_all x2, waiting for transfers between devices, perform_windows_by_axis(): lax.all_to_all(jnp.stack([x_in for _ in range(lax.axis_size(lane_axis))],...  107 us
    all_to_all x2, waiting for transfers between devices, shards(): lax.all_to_all(outgoing, 'inner', split_axis=2, concat_axis=1, tiled=True)  92.9 us
    dot_general x2, matrix products, shards(): jnp.dot(coupling_all, pivot_inverse.T, precision=HIGHEST, preferred_eleme...  66.8 us
    psum x1, waiting for transfers between devices, shards(): lax.psum(lax.psum_scatter(per_front, 'inner', scatter_dimension=1, tiled=...  56.7 us
    reduce_scatter x1, waiting for transfers between devices, shards(): lax.psum_scatter(per_front, 'inner', scatter_dimension=1, tiled=True)  29.8 us
  transfers between devices with their start and end apart: 10, of which 7 were waited for; matrix products, arithmetic and copies ran while one was open for 57% of the time, Pallas kernels for 0%

profile of v1, /device:TPU:96, one launch (start us, length us, event | category | flops | bytes accessed | tf_op | source)
XLA Modules:
  0.0 1097.9 jit_solution(14751144831044171565)
XLA Ops:
  9.7 25.9 %while.14 = (s32[]{:T(128)}, f32[48,128,128]{2,1,0:T(8,128)S(1)}, s32[2048]{0:T(1024)}, bf16[2048,128]{1,0:T(8,128)(2,1)}, s32[]{:T(128)}, /*index=5*/s32[]{:T(128)}, s32[]{:T(128)}, s32[]{:T(128)}) while((s32[]{:T(128)}, f32[48,128,128]{2,1,0:T(8,128)S(1)}, s32[2048]{0:T(1024)}, bf16[2048,128]{1,0:T(8,128)(2,1)}, s32[]{:T(128)}, ...), condition=%wide.region_5.8_spmd.clone, body=%wide.region_4.7_spmd.clone.sunk | while | flops 405823488 | bytes 6737053 | solution.py:173
  60.7 53.7 %all-to-all-done = f32[2,128,16,192]{1,3,0,2:T(8,128)S(1)} async-done(((f32[2,128,16,192]{1,3,0,2:T(8,128)}), f32[2,128,16,192]{1,3,0,2:T(8,128)S(1)}, u32[]{:S(2)}, u32[]{:S(2)}) %all-to-all-start) | async-done | bytes 3145760 | tf_op jit(solution)/shard_map/all_to_all | solution.py:197
  119.1 29.8 %reduce-scatter.2.cloned.1.call-done = f32[6,64,128]{2,1,0:T(8,128)} async-done(((f32[6,1024,128]{2,1,0:T(8,128)}), f32[6,64,128]{2,1,0:T(8,128)}) %reduce-scatter.2.cloned.1.call-update) | async-done | bytes 196624 | tf_op jit(solution)/shard_map/reduce_scatter | solution.py:178
  151.8 56.7 %all-reduce.30.cloned.1.call-done = f32[6,64,128]{2,1,0:T(8,128)} async-done(((f32[6,64,128]{2,1,0:T(8,128)}), f32[6,64,128]{2,1,0:T(8,128)}) %all-reduce.30.cloned.1.call-update) | async-done | bytes 196624 | tf_op jit(solution)/shard_map/psum | solution.py:177
  220.5 71.9 %all-to-all-done.1 = f32[16,64,1024]{2,1,0:T(8,128)} async-done(((f32[16,64,1024]{2,1,0:T(8,128)}), f32[16,64,1024]{2,1,0:T(8,128)}, u32[]{:S(2)}, u32[]{:S(2)}) %all-to-all-start.1) | async-done | bytes 4194336 | tf_op jit(solution)/shard_map/all_to_all | solution.py:16
  297.6 11.7 %cholesky.254 = f32[128,128]{1,0:T(8,128)S(1)} custom-call(f32[128,128]{1,0:T(8,128)S(1)} %get-tuple-element.162), custom_call_target="Cholesky" | custom-call | tf_op jit(solution)/shard_map/jit(cholesky)/cholesky | solution.py:102
  322.9 11.7 %cholesky.265 = f32[128,128]{1,0:T(8,128)S(1)} custom-call(f32[128,128]{1,0:T(8,128)S(1)} %fusion.203), custom_call_target="Cholesky" | custom-call | tf_op jit(solution)/shard_map/jit(cholesky)/cholesky | solution.py:102
  349.8 11.7 %cholesky.276 = f32[128,128]{1,0:T(8,128)S(1)} custom-call(f32[128,128]{1,0:T(8,128)S(1)} %fusion.201), custom_call_target="Cholesky" | custom-call | tf_op jit(solution)/shard_map/jit(cholesky)/cholesky | solution.py:102
  374.2 12.1 %cholesky.287 = f32[128,128]{1,0:T(8,128)S(1)} custom-call(f32[128,128]{1,0:T(8,128)S(1)} %fusion.199), custom_call_target="Cholesky" | custom-call | tf_op jit(solution)/shard_map/jit(cholesky)/cholesky | solution.py:102
  413.5 12.7 %cholesky.298 = f32[128,128]{1,0:T(8,128)S(1)} custom-call(f32[128,128]{1,0:T(8,128)} %fusion.197), custom_call_target="Cholesky" | custom-call | tf_op jit(solution)/shard_map/jit(cholesky)/cholesky | solution.py:102
  428.1 11.3 %custom-call.25 = f32[1,128,128]{1,2,0:T(8,128)} custom-call(f32[1,128,128]{2,1,0:T(8,128)} %get-tuple-element.149), custom_call_target="InvertDiagBlocksLowerTriangular" | custom-call | tf_op jit(solution)/shard_map/jit(_solve_triangular)/triangular_solve | solution.py:104
  447.1 13.2 %cholesky.309 = f32[128,128]{1,0:T(8,128)} custom-call(f32[128,128]{1,0:T(8,128)} %fusion.195), custom_call_target="Cholesky" | custom-call | tf_op jit(solution)/shard_map/jit(cholesky)/cholesky | solution.py:102
  463.9 11.3 %custom-call.26 = f32[1,128,128]{1,2,0:T(8,128)} custom-call(f32[1,128,128]{2,1,0:T(8,128)} %get-tuple-element.147), custom_call_target="InvertDiagBlocksLowerTriangular" | custom-call | tf_op jit(solution)/shard_map/jit(_solve_triangular)/triangular_solve | solution.py:104
  489.3 13.6 %cholesky.320 = f32[128,128]{1,0:T(8,128)} custom-call(f32[128,128]{1,0:T(8,128)} %fusion.193), custom_call_target="Cholesky" | custom-call | tf_op jit(solution)/shard_map/jit(cholesky)/cholesky | solution.py:102
  506.5 11.3 %custom-call.27 = f32[1,128,128]{1,2,0:T(8,128)} custom-call(f32[1,128,128]{2,1,0:T(8,128)} %get-tuple-element.145), custom_call_target="InvertDiagBlocksLowerTriangular" | custom-call | tf_op jit(solution)/shard_map/jit(_solve_triangular)/triangular_solve | solution.py:104
  526.1 13.2 %cholesky.331 = f32[128,128]{1,0:T(8,128)} custom-call(f32[128,128]{1,0:T(8,128)} %fusion.191), custom_call_target="Cholesky" | custom-call | tf_op jit(solution)/shard_map/jit(cholesky)/cholesky | solution.py:102
  542.9 11.3 %custom-call.28 = f32[1,128,128]{1,2,0:T(8,128)} custom-call(f32[1,128,128]{2,1,0:T(8,128)} %get-tuple-element.143), custom_call_target="InvertDiagBlocksLowerTriangular" | custom-call | tf_op jit(solution)/shard_map/jit(_solve_triangular)/triangular_solve | solution.py:104
  568.6 36.2 %fusion.12 = f32[2048,1024]{1,0:T(8,128)S(1)} fusion(f32[2048,1024]{1,0:T(8,128)} %all-gather.3.cloned.1.call-done, f32[512,512]{1,0:T(8,128)S(1)} %copy-done.38, f32[128,128]{1,0:T(8,128)S(1)} %copy-done.86, f32[128,128]{1,0:T(8,128)} %copy-done.82, f32[128,256]{1,0:T(8,128)} %concatenate.310, f32[256,256]{1,0:T(8,128)} %copy-done.78, ...), kind=kOutput, calls=%fused_computation.29 | convolution fusion | flops 25778192384 | bytes 19922944 | tf_op jit(solution)/shard_map/dot_general | solution.py:211
  621.3 18.3 %collective-permute-done.1 = f32[128,2048]{1,0:T(8,128)} collective-permute-done((f32[128,2048]{1,0:T(8,128)}, f32[128,2048]{1,0:T(8,128)}, u32[]{:S(2)}, u32[]{:S(2)}) %collective-permute-start.1) | collective-permute-done | bytes 1048608 | tf_op jit(solution)/shard_map/ppermute | solution.py:30
  659.0 39.2 %all-to-all-done.2 = f32[2,128,16,192]{1,3,0,2:T(8,128)S(1)} async-done(((f32[2,128,16,192]{1,3,0,2:T(8,128)}), f32[2,128,16,192]{1,3,0,2:T(8,128)S(1)}, u32[]{:S(2)}, u32[]{:S(2)}) %all-to-all-start.2) | async-done | bytes 3145760 | tf_op jit(solution)/shard_map/all_to_all | solution.py:197
  737.0 34.9 %all-to-all-done.3 = f32[16,64,1024]{2,1,0:T(8,128)} async-done(((f32[16,64,1024]{2,1,0:T(8,128)}), f32[16,64,1024]{2,1,0:T(8,128)}, u32[]{:S(2)}, u32[]{:S(2)}) %all-to-all-start.3) | async-done | bytes 4194336 | tf_op jit(solution)/shard_map/all_to_all | solution.py:16
  777.1 11.7 %cholesky.342 = f32[128,128]{1,0:T(8,128)S(1)} custom-call(f32[128,128]{1,0:T(8,128)S(1)} %get-tuple-element.160), custom_call_target="Cholesky" | custom-call | tf_op jit(solution)/shard_map/jit(cholesky)/cholesky | solution.py:102
  803.2 11.9 %cholesky.353 = f32[128,128]{1,0:T(8,128)S(1)} custom-call(f32[128,128]{1,0:T(8,128)S(1)} %fusion.187), custom_call_target="Cholesky" | custom-call | tf_op jit(solution)/shard_map/jit(cholesky)/cholesky | solution.py:102
  831.0 11.7 %cholesky.364 = f32[128,128]{1,0:T(8,128)S(1)} custom-call(f32[128,128]{1,0:T(8,128)S(1)} %fusion.185), custom_call_target="Cholesky" | custom-call | tf_op jit(solution)/shard_map/jit(cholesky)/cholesky | solution.py:102
  856.0 12.1 %cholesky.375 = f32[128,128]{1,0:T(8,128)S(1)} custom-call(f32[128,128]{1,0:T(8,128)S(1)} %fusion.183), custom_call_target="Cholesky" | custom-call | tf_op jit(solution)/shard_map/jit(cholesky)/cholesky | solution.py:102
  894.7 11.9 %cholesky.386 = f32[128,128]{1,0:T(8,128)S(1)} custom-call(f32[128,128]{1,0:T(8,128)S(1)} %fusion.181), custom_call_target="Cholesky" | custom-call | tf_op jit(solution)/shard_map/jit(cholesky)/cholesky | solution.py:102
  926.7 13.2 %cholesky.397 = f32[128,128]{1,0:T(8,128)} custom-call(f32[128,128]{1,0:T(8,128)} %fusion.179), custom_call_target="Cholesky" | custom-call | tf_op jit(solution)/shard_map/jit(cholesky)/cholesky | solution.py:102
  943.6 11.3 %custom-call.34 = f32[1,128,128]{1,2,0:T(8,128)} custom-call(f32[1,128,128]{2,1,0:T(8,128)} %get-tuple-element.131), custom_call_target="InvertDiagBlocksLowerTriangular" | custom-call | tf_op jit(solution)/shard_map/jit(_solve_triangular)/triangular_solve | solution.py:104
  969.8 12.5 %cholesky.408 = f32[128,128]{1,0:T(8,128)S(1)} custom-call(f32[128,128]{1,0:T(8,128)} %fusion.177), custom_call_target="Cholesky" | custom-call | tf_op jit(solution)/shard_map/jit(cholesky)/cholesky | solution.py:102
  1002.6 13.2 %cholesky.419 = f32[128,128]{1,0:T(8,128)} custom-call(f32[128,128]{1,0:T(8,128)} %fusion.175), custom_call_target="Cholesky" | custom-call | tf_op jit(solution)/shard_map/jit(cholesky)/cholesky | solution.py:102
  1020.0 11.3 %custom-call.36 = f32[1,128,128]{1,2,0:T(8,128)} custom-call(f32[1,128,128]{2,1,0:T(8,128)} %get-tuple-element.127), custom_call_target="InvertDiagBlocksLowerTriangular" | custom-call | tf_op jit(solution)/shard_map/jit(_solve_triangular)/triangular_solve | solution.py:104
  1049.7 30.6 %fusion.10 = f32[2048,1024]{1,0:T(8,128)S(1)} fusion(f32[2048,1024]{1,0:T(8,128)} %all-gather.5.cloned.1.call-done, f32[512,512]{1,0:T(8,128)S(1)} %copy-done.37, f32[128,128]{1,0:T(8,128)} %copy.413, f32[128,128]{1,0:T(8,128)} %copy-done.81, f32[128,256]{1,0:T(8,128)S(1)} %copy-done.68, f32[256,256]{1,0:T(8,128)} %copy-done.77, f32[256,512]{1,0:T(8,128)} %copy-done.65, ...), kind=kOutput, calls=%fused_computation.23 | convolution fusion | flops 25778192384 | bytes 19922944 | tf_op jit(solution)/shard_map/dot_general | solution.py:211
  (542 shorter events, 444.0 us)
Async XLA Ops:
  7.2 141.7 %reduce-scatter.2.cloned.1.call-start = ((), (), s32[]{:S(2)}) async-start(), calls=%async_computation.5 | async-start | bytes 3342336 | tf_op jit(solution)/shard_map/reduce_scatter | solution.py:178
  9.7 34.9 %collective-permute-start = (f32[128,2048]{0,1:T(8,128)}, f32[128,2048]{0,1:T(8,128)}, u32[]{:S(2)}, u32[]{:S(2)}) collective-permute-start(f32[128,2048]{0,1:T(8,128)} %bitcast.8), channel_id=1, source_target_pairs={{0,16},{16,0},{32,48},{48,32},{64,80},{80,64},{96,112},{112,96},{1... | collective-permute-start | bytes 3145736 | tf_op jit(solution)/shard_map/ppermute | solution.py:30
  39.1 180.7 %copy-start.89 = (s32[24]{0:T(128)}, s32[24]{0:T(128)S(1)}, u32[]{:S(2)}) copy-start(s32[24]{0:T(128)S(1)} %get-tuple-element.175) | copy-start | bytes 292
  53.6 60.9 %all-to-all-start = ((f32[2,128,16,192]{1,3,0,2:T(8,128)}), f32[2,128,16,192]{1,3,0,2:T(8,128)S(1)}, u32[]{:S(2)}, u32[]{:S(2)}) async-start(f32[2,128,16,192]{1,3,0,2:T(8,128)} %pad_maximum_fusion), calls=%async_computation | async-start | bytes 6291456 | tf_op jit(solution)/shard_map/all_to_all | solution.py:197
  60.6 147.9 %all-reduce.30.cloned.1.call-start = ((), (), s32[]{:S(2)}) async-start(), calls=%async_computation.6 | async-start | bytes 393216 | tf_op jit(solution)/shard_map/psum | solution.py:177
  211.8 80.6 %all-to-all-start.1 = ((f32[16,64,1024]{2,1,0:T(8,128)}), f32[16,64,1024]{2,1,0:T(8,128)}, u32[]{:S(2)}, u32[]{:S(2)}) async-start(f32[16,64,1024]{2,1,0:T(8,128)} %stack.31), calls=%async_computation.2 | async-start | bytes 8388608 | tf_op jit(solution)/shard_map/all_to_all | solution.py:16
  218.7 349.9 %all-gather.3.cloned.1.call-start = ((), (), s32[]{:S(2)}) async-start(), calls=%async_computation.7 | async-start | bytes 8912896 | tf_op jit(solution)/shard_map/all_gather | solution.py:209
  346.9 51.4 %copy-start.52 = (f32[128,128]{1,0:T(8,128)}, f32[128,128]{1,0:T(8,128)S(1)}, u32[]{:S(2)}) copy-start(f32[128,128]{1,0:T(8,128)S(1)} %copy.343) | copy-start | bytes 196612
  347.7 25.6 %copy-start.47 = (f32[128,128]{1,0:T(8,128)}, f32[128,128]{1,0:T(8,128)S(1)}, u32[]{:S(2)}) copy-start(f32[128,128]{1,0:T(8,128)S(1)} %convolution_negate_fusion.13) | copy-start | bytes 196612
  349.1 53.6 %copy-start.4 = (f32[256,256]{0,1:T(8,128)}, f32[256,256]{0,1:T(8,128)S(1)}, u32[]{:S(2)}) copy-start(f32[256,256]{0,1:T(8,128)S(1)} %fusion.133) | copy-start | bytes 786436
  373.6 27.5 %copy-start.48 = (f32[128,128]{1,0:T(8,128)S(1)}, f32[128,128]{1,0:T(8,128)}, u32[]{:S(2)}) copy-start(f32[128,128]{1,0:T(8,128)} %copy-done.47) | copy-start | bytes 196612
  373.8 33.7 %copy-start.17 = (f32[128,128]{0,1:T(8,128)}, f32[128,128]{0,1:T(8,128)S(1)}, u32[]{:S(2)}) copy-start(f32[128,128]{0,1:T(8,128)S(1)} %fusion.170) | copy-start | bytes 196612
  401.1 6.4 copy-start.13
  407.6 156.1 %copy-start.2 = (f32[512,512]{0,1:T(8,128)}, f32[512,512]{0,1:T(8,128)S(1)}, u32[]{:S(2)}) copy-start(f32[512,512]{0,1:T(8,128)S(1)} %fusion.51) | copy-start | bytes 3145732
  557.6 6.0 copy-start.24
  557.6 6.0 copy-start.28
  557.7 6.0 copy-start.33
  557.7 6.0 copy-start.58
  558.7 6.9 copy-start.66
  604.8 9.7 copy-start.1
  604.8 9.7 copy-start.88
  604.8 9.7 copy-start.90
  614.5 25.1 %collective-permute-start.1 = (f32[128,2048]{1,0:T(8,128)}, f32[128,2048]{1,0:T(8,128)}, u32[]{:S(2)}, u32[]{:S(2)}) collective-permute-start(f32[128,2048]{1,0:T(8,128)} %convolution_subtract_fusion.1), channel_id=1, source_target_pairs={{0,32},{32,0},{16,48},{48,16},{64,96},{96,64},{80,112},{112,80},{1... | collective-permute-start | bytes 3145736 | tf_op jit(solution)/shard_map/ppermute | solution.py:30
  648.1 50.1 %all-to-all-start.2 = ((f32[2,128,16,192]{1,3,0,2:T(8,128)}), f32[2,128,16,192]{1,3,0,2:T(8,128)S(1)}, u32[]{:S(2)}, u32[]{:S(2)}) async-start(f32[2,128,16,192]{1,3,0,2:T(8,128)} %pad_maximum_fusion.1), calls=%async_computation.3 | async-start | bytes 6291456 | tf_op jit(solution)/shard_map/all_to_all | solution.py:197
  709.1 62.7 %all-to-all-start.3 = ((f32[16,64,1024]{2,1,0:T(8,128)}), f32[16,64,1024]{2,1,0:T(8,128)}, u32[]{:S(2)}, u32[]{:S(2)}) async-start(f32[16,64,1024]{2,1,0:T(8,128)} %stack.36), calls=%async_computation.4 | async-start | bytes 8388608 | tf_op jit(solution)/shard_map/all_to_all | solution.py:16
  715.0 11.6 %copy-start.3 = (f32[512,512]{0,1:T(8,128)S(1)}, f32[512,512]{0,1:T(8,128)}, u32[]{:S(2)}) copy-start(f32[512,512]{0,1:T(8,128)} %copy-done.2) | copy-start | bytes 3145732
  715.0 334.7 %all-gather.5.cloned.1.call-start = ((), (), s32[]{:S(2)}) async-start(), calls=%async_computation.8 | async-start | bytes 8912896 | tf_op jit(solution)/shard_map/all_gather | solution.py:209
  719.1 9.8 copy-start.76
  830.8 52.0 %copy-start.51 = (f32[128,128]{1,0:T(8,128)S(1)}, f32[128,128]{1,0:T(8,128)}, u32[]{:S(2)}) copy-start(f32[128,128]{1,0:T(8,128)} %copy-done.50) | copy-start | bytes 196612
  854.6 33.7 %copy-start.21 = (f32[128,256]{1,0:T(8,128)}, f32[128,256]{1,0:T(8,128)S(1)}, u32[]{:S(2)}) copy-start(f32[128,256]{1,0:T(8,128)S(1)} %concatenate.333) | copy-start | bytes 393220
  1035.6 11.3 %copy-start.65 = (f32[256,512]{1,0:T(8,128)}, f32[256,512]{1,0:T(8,128)S(1)}, u32[]{:S(2)}) copy-start(f32[256,512]{1,0:T(8,128)S(1)} %concatenate.353) | copy-start | bytes 1572868
  1080.4 9.8 copy-start.16
  (69 other events, 198.1 us)
Sparse Core Ops, SparseCore 0:
  37.5 111.3 reduce-scatter.1
  151.2 57.3 all-reduce.29
  222.2 107.4 all-gather.2
  732.0 89.3 all-gather.4
